TPU v7x, 128 devices: a whole 4x4x4 slice. The times are simulated.
128 devices in a mesh: ctx: 16 (over z, y), head: 8 (over x, core).
Axes of the slice: x: 4, y: 4, z: 4, core: 2. Of those that a mesh axis runs over, the one named last changes fastest.
Arguments:
- queries: bfloat16 [32768, 8192], P(('ctx', 'head')), may hold values from -150 to 150
- key_states: bfloat16 [32768, 1024], P(('ctx', 'head')), may hold values from -10 to 10
- value_states: bfloat16 [32768, 1024], P(('ctx', 'head')), may hold values from -6 to 6
- page_ids: int32 [256], replicated, may hold values from 0 to 63, never falling along the last dimension, each value on 1 to 8 neighbouring positions
- ref_group: int32 [256, 4], replicated, may hold values from 0 to 15, all different within a row; in each aligned block of 16 rows (0 to 15, 16 to 31, ...) at most 4 rows name the same one
- ref_slot: int32 [256, 4], replicated, may hold values from 0 to 15
Outputs:
- attended: bfloat16 [32768, 8192], P(('ctx', 'head'))
Inputs may be any that keep to these rules, and one draw needn't show every extreme that they name: `page_ids`: ids never fall; every page has 1 to 8 blocks and one has exactly 8. `ref_group`: a row's 4 values differ; the rows of the 16 blocks of one ctx group name every ctx group exactly 4 times.
All inputs are finite; a program needn't handle non-finite values.
Results may differ from a plain program's by a relative error of at most 0.0042.
Values may be sent and summed in bfloat16 or wider, within the bound.
No kernel may reach another device: no remote copies, remote signals or barrier semaphores. Data moves between devices by JAX's collectives and lax.ppermute only.
A program may use at most 128 MiB of HBM per device.

v0:
```python
import math
import jax
import jax.numpy as jnp
from jax import lax
from jax.sharding import PartitionSpec as P

HD = 128
BLOCK = 128
MAXPAGE = 8


def from_behind(block, axis, distance):
    devices = range(lax.axis_size(axis))
    route = [(i - distance, i) for i in devices if i - distance in devices]
    return lax.ppermute(block, axis, route)


def page_starts(page_ids):
    block_count = page_ids.shape[0]
    position = jnp.arange(block_count, dtype=jnp.int32)
    is_fresh = jnp.concatenate([jnp.ones((1,), dtype=jnp.bool_), page_ids[1:] != page_ids[:-1]])
    return lax.cummax(jnp.where(is_fresh, position, jnp.zeros_like(position)), axis=0)


def allowed_mask(global_block, padded_pages, starts, ref_row, block_size, window):
    nearby = lax.dynamic_slice_in_dim(padded_pages, global_block, window, 0)
    own_page = nearby[window - 1]
    inside = nearby == own_page
    offsets = jnp.arange(window)
    is_last = offsets == window - 1
    rows_at = jnp.arange(block_size)
    causal = rows_at[None, :] <= rows_at[:, None]
    window_ok = inside[None, :, None] & (
        jnp.logical_not(is_last)[None, :, None] | causal[:, None, :]
    )
    window_ok = window_ok.reshape(block_size, window * block_size)
    start_here = lax.dynamic_index_in_dim(starts, global_block, 0, keepdims=False)
    ref_ok = ref_row < start_here
    ref_ok = jnp.broadcast_to(ref_ok[None, :, None], (block_size, ref_row.shape[0], block_size))
    return jnp.concatenate([window_ok, ref_ok.reshape(block_size, -1)], axis=1)


def attend(query_block, key_set, value_set, allowed):
    score_scale = 1.0 / math.sqrt(query_block.shape[-1])
    scores = (
        jnp.einsum("tgqd,sgd->gqts", query_block, key_set, preferred_element_type=jnp.float32)
        * score_scale
    )
    scores = jnp.where(allowed, scores, -1e30)
    row_max = jnp.max(scores, axis=-1, keepdims=True)
    exp_scores = jnp.where(allowed, jnp.exp(scores - row_max), 0.0)
    totals = jnp.sum(exp_scores, axis=-1)
    weights = exp_scores.astype(jnp.bfloat16)
    mixture = jnp.einsum("gqts,sgd->tgqd", weights, value_set, preferred_element_type=jnp.float32)
    return (mixture / jnp.transpose(totals, (2, 0, 1))[..., None]).astype(jnp.bfloat16)


def shards(queries, key_states, value_states, page_ids, ref_group, ref_slot):
    head_queries, head_keys, head_values = (
        lax.all_to_all(queries, "head", split_axis=1, concat_axis=0, tiled=True),
        lax.all_to_all(key_states, "head", split_axis=1, concat_axis=0, tiled=True),
        lax.all_to_all(value_states, "head", split_axis=1, concat_axis=0, tiled=True),
    )
    group_tokens = head_keys.shape[0]
    key_width = head_keys.shape[1]
    local_heads = key_width // HD
    blocks = group_tokens // BLOCK
    reach = MAXPAGE - 1
    refs_count = ref_group.shape[1]
    key_blocks = head_keys.reshape(blocks, BLOCK, key_width)
    value_blocks = head_values.reshape(blocks, BLOCK, key_width)
    tail_keys, tail_values = from_behind(
        (key_blocks[blocks - reach :], value_blocks[blocks - reach :]), "ctx", 1
    )
    near_keys = jnp.concatenate([tail_keys, key_blocks])
    near_values = jnp.concatenate([tail_values, value_blocks])
    ctx_group = lax.axis_index("ctx")
    first_block = ctx_group * blocks
    own_groups = lax.dynamic_slice_in_dim(ref_group, first_block, blocks, 0)
    own_slots = lax.dynamic_slice_in_dim(ref_slot, first_block, blocks, 0)
    own_rows = own_groups * blocks + own_slots
    whole_keys, whole_values = (
        lax.all_gather(key_blocks, "ctx", axis=0, tiled=True),
        lax.all_gather(value_blocks, "ctx", axis=0, tiled=True),
    )
    flat_rows = own_rows.reshape(-1)
    far_keys = jnp.take(whole_keys, flat_rows, axis=0).reshape(blocks, refs_count, BLOCK, key_width)
    far_values = jnp.take(whole_values, flat_rows, axis=0).reshape(
        blocks, refs_count, BLOCK, key_width
    )
    padded_pages = jnp.concatenate([jnp.full((reach,), -1, dtype=jnp.int32), page_ids])
    starts = page_starts(page_ids)
    group_size = head_queries.shape[1] // key_width
    query_blocks = head_queries.reshape(blocks, BLOCK, local_heads, group_size, HD)

    def one_block(local_block):
        global_block = first_block + local_block
        ref_row = lax.dynamic_index_in_dim(own_rows, local_block, 0, keepdims=False)
        key_set = jnp.concatenate(
            [
                lax.dynamic_slice_in_dim(near_keys, local_block, MAXPAGE, 0),
                lax.dynamic_index_in_dim(far_keys, local_block, 0, keepdims=False),
            ]
        )
        value_set = jnp.concatenate(
            [
                lax.dynamic_slice_in_dim(near_values, local_block, MAXPAGE, 0),
                lax.dynamic_index_in_dim(far_values, local_block, 0, keepdims=False),
            ]
        )
        allowed = allowed_mask(global_block, padded_pages, starts, ref_row, BLOCK, MAXPAGE)
        query_block = lax.dynamic_index_in_dim(query_blocks, local_block, 0, keepdims=False)
        return attend(
            query_block,
            key_set.reshape(-1, local_heads, HD),
            value_set.reshape(-1, local_heads, HD),
            allowed,
        )

    outputs = lax.map(one_block, jnp.arange(blocks, dtype=jnp.int32))
    merged = outputs.reshape(group_tokens, head_queries.shape[1])
    return lax.all_to_all(merged, "head", split_axis=0, concat_axis=1, tiled=True)


def solution(mesh):
    placed = (
        P(("ctx", "head"), None),
        P(("ctx", "head"), None),
        P(("ctx", "head"), None),
        P(),
        P(),
        P(),
    )
    return jax.shard_map(
        shards, mesh=mesh, in_specs=placed, out_specs=P(("ctx", "head"), None), check_vma=False
    )
```

profile of v0, /device:TPU:1, one launch (start us, length us, event | category | flops | bytes accessed | tf_op | source)
XLA Modules:
  0.0 519.4 jit_solution(513064871498028624)
XLA Ops:
  7.7 15.0 %all_to_all.67 = bf16[256,8,128]{2,0,1:T(8,128)(2,1)} all-to-all(bf16[256,8,128]{2,0,1:T(8,128)(2,1)S(1)} %copy_bitcast_fusion.4), channel_id=1, replica_groups=mesh['ctx'=16,'head'=8] {'head'}, dimensions={1} | all-to-all | bytes 1048576 | tf_op jit(solution)/shard_map/all_to_all | solution.py:62
  23.9 13.4 %all_to_all.68 = bf16[256,8,128]{2,0,1:T(8,128)(2,1)} all-to-all(bf16[256,8,128]{2,0,1:T(8,128)(2,1)S(1)} %copy_bitcast_fusion.3), channel_id=1, replica_groups=mesh['ctx'=16,'head'=8] {'head'}, dimensions={1} | all-to-all | bytes 1048576 | tf_op jit(solution)/shard_map/all_to_all | solution.py:61
  37.4 4.8 copy.62
  42.2 5.6 %all-to-all-start.2 = ((bf16[256,8,1024]{2,0,1:T(8,128)(2,1)}), bf16[256,8,1024]{2,0,1:T(8,128)(2,1)}, u32[]{:S(2)}, u32[]{:S(2)}) async-start(bf16[256,8,1024]{2,0,1:T(8,128)(2,1)} %bitcast.164), calls=%async_computation.2 | async-start | bytes 8388608 | tf_op jit(solution)/shard_map/all_to_all | solution.py:60
  49.0 3.2 collective-permute-start
  52.3 3.2 collective-permute-start.1
  58.0 8.6 %collective-permute-done.1 = bf16[7,128,128]{2,1,0:T(8,128)(2,1)S(1)} collective-permute-done((bf16[7,128,128]{2,1,0:T(8,128)(2,1)S(1)}, bf16[7,128,128]{2,1,0:T(8,128)(2,1)S(1)}, u32[]{:S(2)}, u32[]{:S(2)}) %collective-permute-start.1) | collective-permute-done | bytes 229408 | tf_op jit(solution)/shard_map/ppermute | solution.py:15
  67.5 29.1 %all-to-all-done.2 = bf16[256,8,1024]{2,0,1:T(8,128)(2,1)} async-done(((bf16[256,8,1024]{2,0,1:T(8,128)(2,1)}), bf16[256,8,1024]{2,0,1:T(8,128)(2,1)}, u32[]{:S(2)}, u32[]{:S(2)}) %all-to-all-start.2) | async-done | bytes 4194336 | tf_op jit(solution)/shard_map/all_to_all | solution.py:60
  96.6 5.2 %copy.54 = bf16[256,8,8,128]{3,2,1,0:T(8,128)(2,1)} copy(bf16[256,8,8,128]{3,1,2,0:T(8,128)(2,1)} %bitcast.50) | data formatting | bytes 8388608
  101.8 4.3 gather_fusion
  106.1 66.7 %all-gather.5.cloned.1.call-done = bf16[256,128,128]{2,1,0:T(8,128)(2,1)} async-done(((bf16[16,128,128]{2,1,0:T(8,128)(2,1)}), bf16[256,128,128]{2,1,0:T(8,128)(2,1)}) %all-gather.5.cloned.1.call-update) | async-done | bytes 8388624 | tf_op jit(solution)/shard_map/all_gather | solution.py:83
  172.9 5.6 %gather_fusion.1 = bf16[64,128,128]{2,1,0:T(8,128)(2,1)} fusion(bf16[256,128,128]{2,1,0:T(8,128)(2,1)} %all-gather.5.cloned.1.call-done, s32[1024]{0:T(1024)S(1)} %pad_clamp_fusion), kind=kCustom, calls=%fused_computation.1.clone | custom fusion | bytes 4194560 | tf_op jit(solution)/shard_map/jit(_take)/gather | solution.py:87
  178.4 4.0 broadcast_select_fusion
  182.4 256.0 %while.10 = (s32[]{:T(128)}, bf16[16,128,1,8,128]{4,3,1,0,2:T(8,128)(2,1)}, s32[16]{0:T(128)S(1)}, bf16[23,128,128]{2,1,0:T(8,128)(2,1)}, bf16[16,4,128,128]{3,2...) while((s32[]{:T(128)}, ...), condition=%wide.region_5.7_spmd, body=%wide.region_2.6_spmd.sunk | while | flops 826882048 | bytes 26014728 | solution.py:120
  194.3 1.5 fusion.41
  195.8 1.7 fusion.42
  210.3 1.5 fusion.41
  211.8 1.7 fusion.42
  226.3 1.5 fusion.41
  227.8 1.7 fusion.42
  242.3 1.5 fusion.41
  243.8 1.7 fusion.42
  258.3 1.5 fusion.41
  259.8 1.7 fusion.42
  274.3 1.5 fusion.41
  275.8 1.7 fusion.42
  290.3 1.5 fusion.41
  291.8 1.7 fusion.42
  306.3 1.5 fusion.41
  307.8 1.7 fusion.42
  322.3 1.5 fusion.41
  323.8 1.7 fusion.42
  338.3 1.5 fusion.41
  339.8 1.7 fusion.42
  354.3 1.5 fusion.41
  355.8 1.7 fusion.42
  370.3 1.5 fusion.41
  371.8 1.7 fusion.42
  386.3 1.5 fusion.41
  387.8 1.7 fusion.42
  402.3 1.5 fusion.41
  403.8 1.7 fusion.42
  419.8 1.7 fusion.42
  435.8 1.7 fusion.42
  438.4 7.3 %all_to_all.59 = bf16[8,256,1024]{2,1,0:T(8,128)(2,1)} reshape(bf16[16,128,1,8,128]{4,3,1,0,2:T(8,128)(2,1)} %get-tuple-element.68) | data formatting | bytes 8388608 | tf_op jit(solution)/shard_map/all_to_all | solution.py:122
  445.8 54.0 %all_to_all.69 = bf16[8,256,1024]{2,1,0:T(8,128)(2,1)} all-to-all(bf16[8,256,1024]{2,1,0:T(8,128)(2,1)} %all_to_all.59), channel_id=1, replica_groups=mesh['ctx'=16,'head'=8] {'head'}, dimensions={0} | all-to-all | bytes 8388608 | tf_op jit(solution)/shard_map/all_to_all | solution.py:122
  499.7 6.5 %copy.41 = bf16[256,8,1024]{0,2,1:T(8,128)(2,1)} copy(bf16[256,8,1024]{2,0,1:T(8,128)(2,1)} %bitcast.165) | data formatting | bytes 8388608 | tf_op jit(solution)/shard_map/all_to_all | solution.py:122
  506.2 6.4 %copy.42 = bf16[256,8192]{1,0:T(8,128)(2,1)} copy(bf16[256,8192]{0,1:T(8,128)(2,1)} %bitcast.166) | data formatting | bytes 8388608 | tf_op jit(solution)/shard_map/all_to_all | solution.py:122
  (382 shorter events, 152.9 us)
Async XLA Ops:
  6.5 1.0 copy-start
  6.5 95.3 %all-gather.3.cloned.1.call-start = ((), (), s32[]{:S(2)}) async-start(), calls=%async_computation.4 | async-start | bytes 8912896 | tf_op jit(solution)/shard_map/all_gather | solution.py:84
  22.7 150.2 %all-gather.5.cloned.1.call-start = ((), (), s32[]{:S(2)}) async-start(), calls=%async_computation.5 | async-start | bytes 8912896 | tf_op jit(solution)/shard_map/all_gather | solution.py:83
  42.1 5.6 %copy-start.5 = (s32[256,4]{0,1:T(4,128)S(1)}, s32[256,4]{0,1:T(4,128)}, u32[]{:S(2)}) copy-start(s32[256,4]{0,1:T(4,128)} %param.15) | copy-start | bytes 12292
  42.1 5.6 %copy-start.6 = (s32[256,4]{0,1:T(4,128)S(1)}, s32[256,4]{0,1:T(4,128)}, u32[]{:S(2)}) copy-start(s32[256,4]{0,1:T(4,128)} %param.14) | copy-start | bytes 12292
  42.2 6.0 %copy-start.4 = (s32[256]{0:T(256)S(1)}, s32[256]{0:T(256)}, u32[]{:S(2)}) copy-start(s32[256]{0:T(256)} %param.13) | copy-start | bytes 3076
  42.2 6.8 %copy-start.2 = (bf16[256,8,128]{2,0,1:T(8,128)(2,1)S(1)}, bf16[256,8,128]{2,0,1:T(8,128)(2,1)}, u32[]{:S(2)}) copy-start(bf16[256,8,128]{2,0,1:T(8,128)(2,1)} %all_to_all.67) | copy-start | bytes 1572868
  42.2 10.1 %copy-start.3 = (bf16[256,8,128]{2,0,1:T(8,128)(2,1)S(1)}, bf16[256,8,128]{2,0,1:T(8,128)(2,1)}, u32[]{:S(2)}) copy-start(bf16[256,8,128]{2,0,1:T(8,128)(2,1)} %all_to_all.68) | copy-start | bytes 1572868
  42.2 54.4 %all-to-all-start.2 = ((bf16[256,8,1024]{2,0,1:T(8,128)(2,1)}), bf16[256,8,1024]{2,0,1:T(8,128)(2,1)}, u32[]{:S(2)}, u32[]{:S(2)}) async-start(bf16[256,8,1024]{2,0,1:T(8,128)(2,1)} %bitcast.164), calls=%async_computation.2 | async-start | bytes 8388608 | tf_op jit(solution)/shard_map/all_to_all | solution.py:60
  49.0 8.0 %collective-permute-start = (bf16[7,128,128]{2,1,0:T(8,128)(2,1)S(1)}, bf16[7,128,128]{2,1,0:T(8,128)(2,1)S(1)}, u32[]{:S(2)}, u32[]{:S(2)}) collective-permute-start(bf16[7,128,128]{2,1,0:T(8,128)(2,1)S(1)} %slice.32), channel_id=1, source_target_pairs={{0,8},{8,16},{16,24},{24,32},{32,40},{40,48},{48,56},{56,64},{64,7... | collective-permute-start | bytes 688136 | tf_op jit(solution)/shard_map/ppermute | solution.py:15
  52.3 14.3 %collective-permute-start.1 = (bf16[7,128,128]{2,1,0:T(8,128)(2,1)S(1)}, bf16[7,128,128]{2,1,0:T(8,128)(2,1)S(1)}, u32[]{:S(2)}, u32[]{:S(2)}) collective-permute-start(bf16[7,128,128]{2,1,0:T(8,128)(2,1)S(1)} %slice.33), channel_id=1, source_target_pairs={{0,8},{8,16},{16,24},{24,32},{32,40},{40,48},{48,56},{56,64},{64,7... | collective-permute-start | bytes 688136 | tf_op jit(solution)/shard_map/ppermute | solution.py:15
  506.2 6.4 %copy-start.1 = (bf16[256,1024]{1,0:T(8,128)(2,1)S(1)}, bf16[256,1024]{1,0:T(8,128)(2,1)}, u32[]{:S(2)}) copy-start(bf16[256,1024]{1,0:T(8,128)(2,1)} %param.12) | copy-start | bytes 1572868
Sparse Core Ops, SparseCore 0:
  22.8 77.1 all-gather.2
  102.2 70.6 all-gather.4
where the time goes:
time: 523 us; the launch traced here: 519 us
  local copies, waits for them, and re-layouts  139 us (27%)
  waiting for transfers between devices  106 us (20%)
  blocking collectives  82.4 us (16%)
  loops' own time  62.4 us (12%)
  other arithmetic  61.2 us (12%)
  matrix products  43.3 us (8%)
  between operations  13.5 us (3%)
  starting transfers between devices  12.1 us (2%)
    all_gather x1, waiting for transfers between devices, shards(): lax.all_gather(key_blocks, 'ctx', axis=0, tiled=True)  66.7 us
    another operation x1, loops' own time, shards(): outputs = lax.map(one_block, jnp.arange(blocks, dtype=jnp.int32))  62.4 us
    all_to_all x1, blocking collectives, shards(): lax.all_to_all(merged, 'head', split_axis=0, concat_axis=1, tiled=True)  54 us
    all_to_all x1, waiting for transfers between devices, shards(): lax.all_to_all(queries, 'head', split_axis=1, concat_axis=0, tiled=True)  29.1 us
    dot_general x16, matrix products, attend(): jnp.einsum('gqts,sgd->tgqd', weights, value_set, preferred_element_type=j...  26.6 us
    reduce_sum x16, other arithmetic, attend(): totals = jnp.sum(exp_scores, axis=-1)  24.1 us
    all_to_all x3, local copies, waits for them, and re-layouts, shards(): lax.all_to_all(merged, 'head', split_axis=0, concat_axis=1, tiled=True)  20.2 us
    dynamic_slice x16, local copies, waits for them, and re-layouts, one_block(): lax.dynamic_slice_in_dim(near_keys, local_block, MAXPAGE, 0)  17.1 us
  transfers between devices with their start and end apart: 5, of which 4 were waited for; matrix products, arithmetic and copies ran while one was open for 4% of the time, Pallas kernels for 0%

commit v1 on v0

--- a/solution.py
+++ b/solution.py
@@ -80,7 +80,9 @@
     own_slots = lax.dynamic_slice_in_dim(ref_slot, first_block, blocks, 0)
     own_rows = own_groups * blocks + own_slots
     whole_keys, whole_values = (
-        lax.all_gather(key_blocks, "ctx", axis=0, tiled=True),
+        jnp.concatenate(
+            lax.all_to_all(jnp.stack([key_blocks] * lax.axis_size("ctx")), "ctx", 0, 0), axis=0
+        ),
         lax.all_gather(value_blocks, "ctx", axis=0, tiled=True),
     )
     flat_rows = own_rows.reshape(-1)

time: 523 us -> 591 us (1.13)
  the two profiles are of different devices: /device:TPU:1 before, /device:TPU:24 now
where the time goes in v1:
time: 591 us; the launch traced here: 587 us
  local copies, waits for them, and re-layouts  144 us (24%)
  waiting for transfers between devices  126 us (21%)
  blocking collectives  123 us (21%)
  other arithmetic  62.8 us (11%)
  loops' own time  56.3 us (10%)
  matrix products  43.4 us (7%)
  starting transfers between devices  18.6 us (3%)
  between operations  13.5 us (2%)
    ppermute x2, waiting for transfers between devices, from_behind(): return lax.ppermute(block, axis, route)  121 us
    another operation x1, loops' own time, shards(): outputs = lax.map(one_block, jnp.arange(blocks, dtype=jnp.int32))  56.3 us
    all_to_all x1, blocking collectives, shards(): lax.all_to_all(queries, 'head', split_axis=1, concat_axis=0, tiled=True)  54.2 us
    all_to_all x1, blocking collectives, shards(): lax.all_to_all(merged, 'head', split_axis=0, concat_axis=1, tiled=True)  54.1 us
    dot_general x16, matrix products, attend(): jnp.einsum('gqts,sgd->tgqd', weights, value_set, preferred_element_type=j...  26.7 us
    reduce_sum x16, other arithmetic, attend(): totals = jnp.sum(exp_scores, axis=-1)  24.3 us
    all_to_all x3, local copies, waits for them, and re-layouts, shards(): lax.all_to_all(merged, 'head', split_axis=0, concat_axis=1, tiled=True)  20.2 us
    dot_general x16, matrix products, attend(): jnp.einsum('tgqd,sgd->gqts', query_block, key_set, preferred_element_type...  16.7 us
  transfers between devices with their start and end apart: 5, of which 3 were waited for; matrix products, arithmetic and copies ran while one was open for 4% of the time, Pallas kernels for 0%

profile of v1, /device:TPU:24, one launch (start us, length us, event | category | flops | bytes accessed | tf_op | source)
XLA Modules:
  0.0 587.3 jit_solution(1694733631973532810)
XLA Ops:
  7.7 14.6 %all_to_all.72 = bf16[256,8,128]{2,0,1:T(8,128)(2,1)} all-to-all(bf16[256,8,128]{2,0,1:T(8,128)(2,1)S(1)} %copy_bitcast_fusion.4), channel_id=1, replica_groups=mesh['ctx'=16,'head'=8] {'head'}, dimensions={1} | all-to-all | bytes 1048576 | tf_op jit(solution)/shard_map/all_to_all | solution.py:62
  22.3 2.0 copy_bitcast_fusion.3
  24.2 3.5 all-to-all-start.1
  27.7 4.8 copy.62
  32.6 5.4 all-to-all-done.1
  38.0 54.2 %all_to_all.73 = bf16[256,8,1024]{2,0,1:T(8,128)(2,1)} all-to-all(bf16[256,8,1024]{2,0,1:T(8,128)(2,1)} %bitcast.166), channel_id=1, replica_groups=mesh['ctx'=16,'head'=8] {'head'}, dimensions={1} | all-to-all | bytes 8388608 | tf_op jit(solution)/shard_map/all_to_all | solution.py:60
  92.2 5.4 stack.3
  97.5 8.3 %all-to-all-start.2 = ((bf16[16,16,128,128]{3,2,1,0:T(8,128)(2,1)}), bf16[16,16,128,128]{3,2,1,0:T(8,128)(2,1)}, u32[]{:S(2)}, u32[]{:S(2)}) async-start(bf16[16,16,128,128]{3,2,1,0:T(8,128)(2,1)} %stack.3), calls=%async_computation.2 | async-start | bytes 16777216 | tf_op jit(solution)/shard_map/all_to_all | solution.py:84
  107.1 3.4 collective-permute-start
  110.5 3.4 collective-permute-start.1
  113.9 118.6 %collective-permute-done = bf16[7,128,128]{2,1,0:T(8,128)(2,1)S(1)} collective-permute-done((bf16[7,128,128]{2,1,0:T(8,128)(2,1)S(1)}, bf16[7,128,128]{2,1,0:T(8,128)(2,1)S(1)}, u32[]{:S(2)}, u32[]{:S(2)}) %collective-permute-start) | collective-permute-done | bytes 229408 | tf_op jit(solution)/shard_map/ppermute | solution.py:15
  233.4 2.3 collective-permute-done.1
  235.8 5.2 copy.54
  241.0 4.3 gather_fusion.1
  245.4 5.5 gather_fusion
  250.9 4.0 broadcast_select_fusion
  254.9 251.2 %while.10 = (s32[]{:T(128)}, bf16[16,128,1,8,128]{4,3,1,0,2:T(8,128)(2,1)}, s32[16]{0:T(128)S(1)}, bf16[23,128,128]{2,1,0:T(8,128)(2,1)}, bf16[16,4,128,128]{3,2...) while((s32[]{:T(128)}, ...), condition=%wide.region_5.7_spmd, body=%wide.region_2.6_spmd.sunk | while | flops 826882048 | bytes 26014728 | solution.py:122
  266.5 1.5 fusion.41
  268.0 1.7 fusion.42
  282.2 1.5 fusion.41
  283.7 1.7 fusion.42
  297.9 1.5 fusion.41
  299.4 1.7 fusion.42
  313.6 1.5 fusion.41
  315.1 1.7 fusion.42
  329.3 1.5 fusion.41
  330.8 1.7 fusion.42
  346.5 1.7 fusion.42
  362.2 1.7 fusion.42
  377.9 1.7 fusion.42
  392.1 1.5 fusion.41
  393.6 1.7 fusion.42
  407.7 1.5 fusion.41
  409.3 1.7 fusion.42
  423.4 1.5 fusion.41
  425.0 1.7 fusion.42
  439.1 1.5 fusion.41
  440.7 1.7 fusion.42
  454.8 1.5 fusion.41
  456.4 1.7 fusion.42
  470.5 1.5 fusion.41
  472.1 1.7 fusion.42
  487.8 1.7 fusion.42
  503.5 1.7 fusion.42
  506.1 7.3 %all_to_all.63 = bf16[8,256,1024]{2,1,0:T(8,128)(2,1)} reshape(bf16[16,128,1,8,128]{4,3,1,0,2:T(8,128)(2,1)} %get-tuple-element.68) | data formatting | bytes 8388608 | tf_op jit(solution)/shard_map/all_to_all | solution.py:124
  513.4 54.1 %all_to_all.74 = bf16[8,256,1024]{2,1,0:T(8,128)(2,1)} all-to-all(bf16[8,256,1024]{2,1,0:T(8,128)(2,1)} %all_to_all.63), channel_id=1, replica_groups=mesh['ctx'=16,'head'=8] {'head'}, dimensions={0} | all-to-all | bytes 8388608 | tf_op jit(solution)/shard_map/all_to_all | solution.py:124
  567.6 6.5 %copy.41 = bf16[256,8,1024]{0,2,1:T(8,128)(2,1)} copy(bf16[256,8,1024]{2,0,1:T(8,128)(2,1)} %bitcast.167) | data formatting | bytes 8388608 | tf_op jit(solution)/shard_map/all_to_all | solution.py:124
  574.1 6.4 %copy.42 = bf16[256,8192]{1,0:T(8,128)(2,1)} copy(bf16[256,8192]{0,1:T(8,128)(2,1)} %bitcast.168) | data formatting | bytes 8388608 | tf_op jit(solution)/shard_map/all_to_all | solution.py:124
  (380 shorter events, 154.9 us)
Async XLA Ops:
  6.5 1.0 copy-start
  6.5 238.8 %all-gather.2.cloned.1.call-start = ((), (), s32[]{:S(2)}) async-start(), calls=%async_computation.5 | async-start | bytes 8912896 | tf_op jit(solution)/shard_map/all_gather | solution.py:86
  24.2 13.7 %all-to-all-start.1 = ((bf16[256,8,128]{2,0,1:T(8,128)(2,1)}), bf16[256,8,128]{2,0,1:T(8,128)(2,1)S(1)}, u32[]{:S(2)}, u32[]{:S(2)}) async-start(bf16[256,8,128]{2,0,1:T(8,128)(2,1)} %copy_bitcast_fusion.3), calls=%async_computation.1 | async-start | bytes 1048576 | tf_op jit(solution)/shard_map/all_to_all | solution.py:61
  97.5 8.3 %copy-start.4 = (s32[256,4]{0,1:T(4,128)S(1)}, s32[256,4]{0,1:T(4,128)}, u32[]{:S(2)}) copy-start(s32[256,4]{0,1:T(4,128)} %param.15) | copy-start | bytes 12292
  97.5 8.3 %copy-start.5 = (s32[256,4]{0,1:T(4,128)S(1)}, s32[256,4]{0,1:T(4,128)}, u32[]{:S(2)}) copy-start(s32[256,4]{0,1:T(4,128)} %param.14) | copy-start | bytes 12292
  97.5 8.7 %copy-start.3 = (s32[256]{0:T(256)S(1)}, s32[256]{0:T(256)}, u32[]{:S(2)}) copy-start(s32[256]{0:T(256)} %param.13) | copy-start | bytes 3076
  97.5 9.6 %copy-start.2 = (bf16[256,8,128]{2,0,1:T(8,128)(2,1)S(1)}, bf16[256,8,128]{2,0,1:T(8,128)(2,1)}, u32[]{:S(2)}) copy-start(bf16[256,8,128]{2,0,1:T(8,128)(2,1)} %all_to_all.72) | copy-start | bytes 1572868
  97.5 143.5 %all-to-all-start.2 = ((bf16[16,16,128,128]{3,2,1,0:T(8,128)(2,1)}), bf16[16,16,128,128]{3,2,1,0:T(8,128)(2,1)}, u32[]{:S(2)}, u32[]{:S(2)}) async-start(bf16[16,16,128,128]{3,2,1,0:T(8,128)(2,1)} %stack.3), calls=%async_computation.2 | async-start | bytes 16777216 | tf_op jit(solution)/shard_map/all_to_all | solution.py:84
  107.1 125.4 %collective-permute-start = (bf16[7,128,128]{2,1,0:T(8,128)(2,1)S(1)}, bf16[7,128,128]{2,1,0:T(8,128)(2,1)S(1)}, u32[]{:S(2)}, u32[]{:S(2)}) collective-permute-start(bf16[7,128,128]{2,1,0:T(8,128)(2,1)S(1)} %slice.32), channel_id=1, source_target_pairs={{0,8},{8,16},{16,24},{24,32},{32,40},{40,48},{48,56},{56,64},{64,7... | collective-permute-start | bytes 688136 | tf_op jit(solution)/shard_map/ppermute | solution.py:15
  110.5 125.2 %collective-permute-start.1 = (bf16[7,128,128]{2,1,0:T(8,128)(2,1)S(1)}, bf16[7,128,128]{2,1,0:T(8,128)(2,1)S(1)}, u32[]{:S(2)}, u32[]{:S(2)}) collective-permute-start(bf16[7,128,128]{2,1,0:T(8,128)(2,1)S(1)} %slice.33), channel_id=1, source_target_pairs={{0,8},{8,16},{16,24},{24,32},{32,40},{40,48},{48,56},{56,64},{64,7... | collective-permute-start | bytes 688136 | tf_op jit(solution)/shard_map/ppermute | solution.py:15
  574.1 6.4 %copy-start.1 = (bf16[256,1024]{1,0:T(8,128)(2,1)S(1)}, bf16[256,1024]{1,0:T(8,128)(2,1)}, u32[]{:S(2)}) copy-start(bf16[256,1024]{1,0:T(8,128)(2,1)} %param.12) | copy-start | bytes 1572868
Sparse Core Ops, SparseCore 0:
  22.4 71.1 all-gather.1
